TPU v7x, 256 devices: a whole 4x4x8 slice. The times are simulated.
256 devices in a mesh: seq: 8 (over z_lo, x), chan: 32 (over y, z_hi, core).
Axes of the slice: x: 4, y: 4, z: 8 (z_hi: 4, z_lo: 2; z = z_hi * 2 + z_lo), core: 2. Of those that a mesh axis runs over, the one named last changes fastest.
Arguments:
- tokens: bfloat16 [8192, 4096], P('seq', 'chan'), may hold values from -6 to 6
- in_weight: bfloat16 [4096, 3, 4096], P(None, None, 'chan'), may hold values from -0.09375 to 0.09375
- short_taps: float32 [3, 3, 4096], P(None, None, 'chan'), may hold values from -3 to 3
- filter_taps: float32 [8192, 4096], P('seq', 'chan'), may hold values from -1 to 1
- skip_gain: float32 [4096], P('chan'), may hold values from -4 to 4
- out_weight: bfloat16 [4096, 4096], P('chan'), may hold values from -0.1875 to 0.1875
Outputs:
- layer_out: bfloat16 [8192, 4096], P('seq', 'chan')
All inputs are finite; a program needn't handle non-finite values.
Results may differ from a plain program's by a relative error of at most 0.007.
Values may be sent and summed in bfloat16 or wider, within the bound.
No kernel may reach another device: no remote copies, remote signals or barrier semaphores. Data moves between devices by JAX's collectives and lax.ppermute only.
A program may use at most 128 MiB of HBM per device.

v0:
```python
import math
import jax
import jax.numpy as jnp
from jax import lax
from jax.sharding import PartitionSpec as P

COLS = 256
highest = lax.Precision.HIGHEST


def from_behind(shard, axis, by):
    size = lax.axis_size(axis)
    pairs = [(i, i + by) for i in range(size) if 0 <= i + by < size]
    return lax.ppermute(shard, axis, pairs)


def phase_table(row_count, col_count, period):
    row_index = jnp.arange(row_count, dtype=jnp.int32)[:, None]
    col_index = jnp.arange(col_count, dtype=jnp.int32)[None, :]
    angle = (row_index * col_index % period).astype(jnp.float32) * (2.0 * math.pi / period)
    return (jnp.cos(angle), jnp.sin(angle))


def real_transform(signal, cosine, sines, pattern):
    real_part = jnp.einsum(pattern, cosine, signal, precision=highest)
    imag_part = -jnp.einsum(pattern, sines, signal, precision=highest)
    return (real_part, imag_part)


def complex_transform(real_part, imag_part, cosine, sines, direction, pattern):
    cos_real = jnp.einsum(pattern, cosine, real_part, precision=highest)
    cos_imag = jnp.einsum(pattern, cosine, imag_part, precision=highest)
    sin_real = jnp.einsum(pattern, sines, real_part, precision=highest)
    sin_imag = jnp.einsum(pattern, sines, imag_part, precision=highest)
    return (cos_real - direction * sin_imag, cos_imag + direction * sin_real)


def rotate(real_part, imag_part, cosine, sines, direction):
    return (
        real_part * cosine - direction * imag_part * sines,
        imag_part * cosine + direction * real_part * sines,
    )


def spectrum_product(real_part, imag_part):
    prod_real = real_part[0] * real_part[1] - imag_part[0] * imag_part[1]
    prod_imag = real_part[0] * imag_part[1] + imag_part[0] * real_part[1]
    return (prod_real[None], prod_imag[None])


def real_inverse(real_part, imag_part, cosine, sines, pattern, length):
    return (
        jnp.einsum(pattern, cosine, real_part, precision=highest)
        - jnp.einsum(pattern, sines, imag_part, precision=highest)
    ) / length


def channel_convolve(signal, filter_taps):
    stacked = jnp.stack([signal, filter_taps])
    whole_seq = lax.all_to_all(stacked, "seq", split_axis=2, concat_axis=1, tiled=True)
    length = whole_seq.shape[1]
    narrow = whole_seq.shape[2]
    full_rows = 2 * length // COLS
    half_rows = full_rows // 2
    period = 2 * length
    laid_out = whole_seq.reshape(2, half_rows, COLS, narrow)
    first_cos, first_sin = phase_table(full_rows, half_rows, full_rows)
    real_part, imag_part = real_transform(laid_out, first_cos, first_sin, "kn,xnmc->xkmc")
    twist_cos, twist_sin = phase_table(full_rows, COLS, period)
    twist_cos = twist_cos[:, :, None]
    twist_sin = twist_sin[:, :, None]
    real_part, imag_part = rotate(real_part, imag_part, twist_cos, twist_sin, -1.0)
    second_cos, second_sin = phase_table(COLS, COLS, COLS)
    pattern = "kn,xanc->xakc"
    real_part, imag_part = complex_transform(
        real_part, imag_part, second_cos, second_sin, -1.0, pattern
    )
    real_part, imag_part = spectrum_product(real_part, imag_part)
    real_part, imag_part = complex_transform(
        real_part, imag_part, second_cos, second_sin, 1.0, pattern
    )
    real_part, imag_part = rotate(real_part, imag_part, twist_cos, twist_sin, 1.0)
    last_cos, last_sin = phase_table(half_rows, full_rows, full_rows)
    values = real_inverse(real_part, imag_part, last_cos, last_sin, "nk,xkmc->xnmc", period)
    values = values.reshape(length, narrow)
    return lax.all_to_all(values, "seq", split_axis=0, concat_axis=1, tiled=True)


def body(tokens, in_weight, short_taps, filter_taps, skip_gain, out_weight):
    tok_count = tokens.shape[0]
    chan_count = in_weight.shape[2]
    flat_weight = in_weight.reshape(in_weight.shape[0], 3 * chan_count)
    projected = jnp.dot(
        lax.all_gather(tokens, "chan", axis=1, tiled=True),
        flat_weight,
        preferred_element_type=jnp.float32,
    )
    projected = projected.astype(jnp.bfloat16).reshape(tok_count, 3, chan_count)
    previous = from_behind(projected[-2:], "seq", 1)
    extended = jnp.concatenate([previous, projected], axis=0).astype(jnp.float32)
    short_mixed = (
        short_taps[0] * extended[2:]
        + short_taps[1] * extended[1:-1]
        + short_taps[2] * extended[:-2]
    )
    gate_out = short_mixed[:, 0]
    signal = short_mixed[:, 1] * short_mixed[:, 2]
    convolved = channel_convolve(signal, filter_taps)
    hidden = (gate_out * (convolved + skip_gain * signal)).astype(jnp.bfloat16)
    partial_terms = jnp.dot(hidden, out_weight, preferred_element_type=jnp.float32)
    layer_out = lax.psum_scatter(partial_terms, "chan", scatter_dimension=1, tiled=True)
    return layer_out.astype(jnp.bfloat16)


def solution(mesh):
    in_specs = (
        P("seq", "chan"),
        P(None, None, "chan"),
        P(None, None, "chan"),
        P("seq", "chan"),
        P("chan"),
        P("chan", None),
    )
    out_specs = P("seq", "chan")
    return jax.shard_map(body, mesh=mesh, in_specs=in_specs, out_specs=out_specs, check_vma=False)
```

profile of v0, /device:TPU:6, one launch (start us, length us, event | category | flops | bytes accessed | tf_op | source)
XLA Modules:
  0.0 368.0 jit_solution(10557821155383948905)
XLA Ops:
  6.5 0.0 copy-start
  6.5 0.0 all-gather.2.cloned.1.call-start
  6.5 0.7 all-gather.2.cloned.1.call-update
  7.3 4.8 %copy.29 = bf16[4096,3,128]{0,2,1:T(8,128)(2,1)} copy(bf16[4096,3,128]{2,0,1:T(8,128)(2,1)} %param.7) | data formatting | bytes 6291456 | tf_op args[1]
  12.0 84.9 %all-gather.2.cloned.1.call-done = bf16[1024,4096]{1,0:T(8,128)(2,1)} async-done(((bf16[1024,128]{1,0:T(8,128)(2,1)}), bf16[1024,4096]{1,0:T(8,128)(2,1)}) %all-gather.2.cloned.1.call-update) | async-done | bytes 8388624 | tf_op jit(solution)/shard_map/all_gather | solution.py:94
  97.0 0.0 copy-start.3
  97.0 0.0 copy-start.2
  97.0 8.8 %convolution_convert_fusion = bf16[1024,384]{1,0:T(8,128)(2,1)S(1)} fusion(bf16[1024,4096]{1,0:T(8,128)(2,1)} %all-gather.2.cloned.1.call-done, bf16[4096,384]{0,1:T(8,128)(2,1)} %bitcast.137), kind=kOutput, calls=%fused_computation.21 | convolution fusion | flops 3221618688 | bytes 12320768 | tf_op jit(solution)/shard_map/dot_general | solution.py:93
  105.8 1.9 collective-permute-start
  107.8 0.0 copy-done.3
  107.8 0.0 copy-done.2
  107.8 0.2 copy.32
  108.0 0.3 copy.30
  108.3 3.0 collective-permute-done
  111.3 0.2 copy.31
  111.5 0.4 maximum_convert_fusion
  111.9 1.2 fusion.14
  113.1 0.1 fusion.45
  113.1 0.1 pad_maximum_fusion
  113.2 1.8 copy.33
  115.0 4.8 %all-to-all-start = ((f32[2,1024,128]{1,0,2:T(2,128)}), f32[2,1024,128]{1,0,2:T(2,128)}, u32[]{:S(2)}, u32[]{:S(2)}) async-start(f32[2,1024,128]{1,0,2:T(2,128)} %copy.33), calls=%async_computation | async-start | bytes 2097152 | tf_op jit(solution)/shard_map/all_to_all | solution.py:60
  119.8 0.5 reduce-scatter.2.cloned.1.call-start
  120.3 0.3 fusion.62
  120.6 0.3 broadcast_multiply_fusion
  120.8 11.4 %all-to-all-done = f32[2,1024,128]{1,0,2:T(2,128)} async-done(((f32[2,1024,128]{1,0,2:T(2,128)}), f32[2,1024,128]{1,0,2:T(2,128)}, u32[]{:S(2)}, u32[]{:S(2)}) %all-to-all-start) | async-done | bytes 1048608 | tf_op jit(solution)/shard_map/all_to_all | solution.py:60
  132.3 1.6 copy.34
  133.8 1.6 copy.35
  135.4 2.5 reshape.85
  137.9 0.0 copy-start.1
  137.9 3.2 fusion.70
  141.2 0.0 copy-done.1
  141.2 2.4 fusion
  143.6 3.8 %fusion.2 = f32[2,64,16,256]{3,2,1,0:T(8,128)S(1)} fusion(f32[2,64,256,16]{2,1,3,0:T(8,128)S(1)} %get-tuple-element.6), kind=kOutput, calls=%fused_computation.8 | convolution fusion | flops 1611530240 | bytes 4194304 | tf_op jit(solution)/shard_map/kn,xanc->xakc/dot_general | solution.py:32
  147.4 4.0 %fusion.4 = f32[2,64,16,256]{3,2,1,0:T(8,128)S(1)} fusion(f32[2,64,256,16]{2,1,3,0:T(8,128)S(1)} %get-tuple-element.6), kind=kOutput, calls=%fused_computation.10 | convolution fusion | flops 1611530240 | bytes 4194304 | tf_op jit(solution)/shard_map/kn,xanc->xakc/dot_general | solution.py:34
  151.4 3.9 %subtract_bitcast_fusion = f32[2,64,256,16]{2,3,1,0:T(8,128)S(1)} fusion(f32[2,64,16,256]{3,2,1,0:T(8,128)S(1)} %fusion.4, f32[2,64,256,16]{2,1,3,0:T(8,128)S(1)} %get-tuple-element.5), kind=kOutput, calls=%fused_computation.7 | convolution fusion | flops 1612578816 | bytes 6291456 | tf_op jit(solution)/shard_map/kn,xanc->xakc/dot_general | solution.py:31
  155.4 3.9 %add_bitcast_fusion = f32[2,64,256,16]{2,3,1,0:T(8,128)S(1)} fusion(f32[2,64,16,256]{3,2,1,0:T(8,128)S(1)} %fusion.2, f32[2,64,256,16]{2,1,3,0:T(8,128)S(1)} %get-tuple-element.5), kind=kOutput, calls=%fused_computation.6 | convolution fusion | flops 1612578816 | bytes 6291456 | tf_op jit(solution)/shard_map/kn,xanc->xakc/dot_general | solution.py:33
  159.2 0.6 multiply_subtract_fusion
  159.8 2.0 fusion.24
  161.8 2.2 fusion.20
  164.0 2.0 fusion.16
  166.0 2.1 add_bitcast_fusion.1
  168.1 1.3 fusion.27
  169.5 2.1 fusion.19
  171.6 0.0 copy-start.4
  171.6 1.2 all_to_all.28
  172.8 0.3 copy.42
  173.1 12.9 %all_to_all.34 = f32[8,1024,16]{1,2,0:T(8,128)S(1)} all-to-all(f32[8,1024,16]{1,2,0:T(8,128)S(1)} %copy.42), channel_id=1, replica_groups=mesh['seq'=8,'chan'=32] {'seq'}, dimensions={0} | all-to-all | bytes 1048576 | tf_op jit(solution)/shard_map/all_to_all | solution.py:86
  186.1 0.0 copy-done.4
  186.1 0.1 fusion.30
  186.2 0.0 copy-done
  186.2 8.1 %fusion.142 = f32[1024,4096]{1,0:T(8,128)} fusion(bf16[1024,128]{0,1:T(8,128)(2,1)S(1)} %fusion.30, bf16[128,4096]{1,0:T(8,128)(2,1)S(1)} %copy-done), kind=kOutput, calls=%fused_computation.161 | convolution fusion | flops 1073741824 | bytes 18087936 | tf_op jit(solution)/shard_map/dot_general | solution.py:110
  194.3 0.0 reduce-scatter.2.cloned.1.call-update
  194.4 164.8 %reduce-scatter.2.cloned.1.call-done = f32[1024,128]{1,0:T(8,128)} async-done(((f32[1024,4096]{1,0:T(8,128)}), f32[1024,128]{1,0:T(8,128)}) %reduce-scatter.2.cloned.1.call-update) | async-done | bytes 524304 | tf_op jit(solution)/shard_map/reduce_scatter | solution.py:111
  359.2 1.8 convert_element_type.67
  (3 shorter events, 0.0 us)
Async XLA Ops:
  6.5 179.7 %copy-start = (bf16[128,4096]{1,0:T(8,128)(2,1)S(1)}, bf16[128,4096]{1,0:T(8,128)(2,1)}, u32[]{:S(2)}) copy-start(bf16[128,4096]{1,0:T(8,128)(2,1)} %param.11) | copy-start | bytes 3145732
  6.5 90.4 %all-gather.2.cloned.1.call-start = ((), (), s32[]{:S(2)}) async-start(), calls=%async_computation.3 | async-start | bytes 8650752 | tf_op jit(solution)/shard_map/all_gather | solution.py:94
  97.0 10.8 %copy-start.3 = (f32[3,3,128]{2,1,0:T(4,128)S(1)}, f32[3,3,128]{2,1,0:T(4,128)}, u32[]{:S(2)}) copy-start(f32[3,3,128]{2,1,0:T(4,128)} %param.8) | copy-start | bytes 13828
  97.0 10.8 %copy-start.2 = (f32[1024,128]{1,0:T(8,128)S(1)}, f32[1024,128]{1,0:T(8,128)}, u32[]{:S(2)}) copy-start(f32[1024,128]{1,0:T(8,128)} %param.9) | copy-start | bytes 1572868
  105.8 5.5 %collective-permute-start = (bf16[2,3,128]{2,1,0:T(4,128)(2,1)S(1)}, bf16[2,3,128]{2,1,0:T(4,128)(2,1)S(1)}, u32[]{:S(2)}, u32[]{:S(2)}) collective-permute-start(bf16[2,3,128]{2,1,0:T(4,128)(2,1)S(1)} %slice.51), channel_id=1, source_target_pairs={{0,32},{32,64},{64,96},{96,128},{128,160},{160,192},{192,224},{1,3... | collective-permute-start | bytes 4616 | tf_op jit(solution)/shard_map/ppermute | solution.py:14
  115.0 17.3 %all-to-all-start = ((f32[2,1024,128]{1,0,2:T(2,128)}), f32[2,1024,128]{1,0,2:T(2,128)}, u32[]{:S(2)}, u32[]{:S(2)}) async-start(f32[2,1024,128]{1,0,2:T(2,128)} %copy.33), calls=%async_computation | async-start | bytes 2097152 | tf_op jit(solution)/shard_map/all_to_all | solution.py:60
  119.8 239.3 %reduce-scatter.2.cloned.1.call-start = ((), (), s32[]{:S(2)}) async-start(), calls=%async_computation.4 | async-start | bytes 17301504 | tf_op jit(solution)/shard_map/reduce_scatter | solution.py:111
  137.9 3.2 copy-start.1
  171.6 14.5 %copy-start.4 = (f32[128]{0:T(128)S(1)}, f32[128]{0:T(128)}, u32[]{:S(2)}) copy-start(f32[128]{0:T(128)} %param.10) | copy-start | bytes 1540
Sparse Core Ops, SparseCore 0:
  9.8 87.1 all-gather.1
  194.5 164.6 reduce-scatter.1
where the time goes:
time: 374 us; the launch traced here: 368 us
  waiting for transfers between devices  265 us (71%)
  matrix products  49.9 us (13%)
  local copies, waits for them, and re-layouts  14.5 us (4%)
  between operations  13.8 us (4%)
  blocking collectives  12.9 us (3%)
  starting transfers between devices  7.19 us (2%)
  other arithmetic  4.7 us (1%)
    reduce_scatter x1, waiting for transfers between devices, body(): lax.psum_scatter(partial_terms, 'chan', scatter_dimension=1, tiled=True)  165 us
    all_gather x1, waiting for transfers between devices, body(): lax.all_gather(tokens, 'chan', axis=1, tiled=True)  84.9 us
    all_to_all x1, blocking collectives, channel_convolve(): lax.all_to_all(values, 'seq', split_axis=0, concat_axis=1, tiled=True)  12.9 us
    all_to_all x1, waiting for transfers between devices, channel_convolve(): lax.all_to_all(stacked, 'seq', split_axis=2, concat_axis=1, tiled=True)  11.4 us
    dot_general x1, matrix products, body(): jnp.dot(lax.all_gather(tokens, 'chan', axis=1, tiled=True), flat_weight,...  8.84 us
    dot_general x1, matrix products, body(): jnp.dot(hidden, out_weight, preferred_element_type=jnp.float32)  8.12 us
  transfers between devices with their start and end apart: 4, of which 4 were waited for; matrix products, arithmetic and copies ran while one was open for 2% of the time, Pallas kernels for 0%

commit v1 on v0

--- a/solution.py
+++ b/solution.py
@@ -91,7 +91,9 @@
     chan_count = in_weight.shape[2]
     flat_weight = in_weight.reshape(in_weight.shape[0], 3 * chan_count)
     projected = jnp.dot(
-        lax.all_gather(tokens, "chan", axis=1, tiled=True),
+        jnp.concatenate(
+            lax.all_to_all(jnp.stack([tokens] * lax.axis_size("chan")), "chan", 0, 0), axis=1
+        ),
         flat_weight,
         preferred_element_type=jnp.float32,
     )

time: 374 us -> 487 us (1.30)
  waiting for transfers between devices: 265 us -> 351 us
  starting transfers between devices: 7.19 us -> 27.3 us
  local copies, waits for them, and re-layouts: 14.5 us -> 19.9 us
    all_to_all x0 -> x1, waiting for transfers between devices: none -> 177 us  [body(): lax.all_to_all(jnp.stack([tokens] * lax.axis_size('chan')), 'chan', 0, 0)]
    all_gather x1 -> x0, waiting for transfers between devices: 84.9 us -> none  [body(): lax.all_gather(tokens, 'chan', axis=1, tiled=True)]
    all_to_all x0 -> x1, starting transfers between devices: none -> 11.6 us  [body(): lax.all_to_all(jnp.stack([tokens] * lax.axis_size('chan')), 'chan', 0, 0)]
    ppermute x1, starting transfers between devices: 1.92 us -> 8.62 us  [from_behind(): return lax.ppermute(shard, axis, pairs)]
  transfers between devices with their start and end apart: 4 -> 4, of which waited for: 4 -> 4; matrix products, arithmetic and copies ran while one was open for 2% -> 1% of each run, Pallas kernels for 0% -> 0%
where the time goes in v1:
time: 487 us; the launch traced here: 480 us
  waiting for transfers between devices  351 us (72%)
  matrix products  50 us (10%)
  starting transfers between devices  27.3 us (6%)
  local copies, waits for them, and re-layouts  19.9 us (4%)
  between operations  13.9 us (3%)
  blocking collectives  12.6 us (3%)
    all_to_all x1, waiting for transfers between devices, body(): lax.all_to_all(jnp.stack([tokens] * lax.axis_size('chan')), 'chan', 0, 0)  177 us
    reduce_scatter x1, waiting for transfers between devices, body(): lax.psum_scatter(partial_terms, 'chan', scatter_dimension=1, tiled=True)  163 us
    all_to_all x1, blocking collectives, channel_convolve(): lax.all_to_all(values, 'seq', split_axis=0, concat_axis=1, tiled=True)  12.6 us
    all_to_all x1, starting transfers between devices, body(): lax.all_to_all(jnp.stack([tokens] * lax.axis_size('chan')), 'chan', 0, 0)  11.6 us
    all_to_all x1, waiting for transfers between devices, channel_convolve(): lax.all_to_all(stacked, 'seq', split_axis=2, concat_axis=1, tiled=True)  10.7 us
  transfers between devices with their start and end apart: 4, of which 4 were waited for; matrix products, arithmetic and copies ran while one was open for 1% of the time, Pallas kernels for 0%

profile of v1, /device:TPU:6, one launch (start us, length us, event | category | flops | bytes accessed | tf_op | source)
XLA Modules:
  0.0 479.6 jit_solution(145103597572445957)
XLA Ops:
  6.5 0.0 copy-start
  6.5 1.2 copy.30
  7.7 4.3 stack.6
  12.0 11.6 %all-to-all-start = ((bf16[32,1024,128]{1,2,0:T(8,128)(2,1)}), bf16[32,1024,128]{1,2,0:T(8,128)(2,1)}, u32[]{:S(2)}, u32[]{:S(2)}) async-start(bf16[32,1024,128]{1,2,0:T(8,128)(2,1)} %stack.6), calls=%async_computation | async-start | bytes 16777216 | tf_op jit(solution)/shard_map/all_to_all | solution.py:95
  23.7 4.7 copy.31
  28.4 177.3 %all-to-all-done = bf16[32,1024,128]{1,2,0:T(8,128)(2,1)} async-done(((bf16[32,1024,128]{1,2,0:T(8,128)(2,1)}), bf16[32,1024,128]{1,2,0:T(8,128)(2,1)}, u32[]{:S(2)}, u32[]{:S(2)}) %all-to-all-start) | async-done | bytes 8388640 | tf_op jit(solution)/shard_map/all_to_all | solution.py:95
  205.7 0.0 copy-start.3
  205.7 0.0 copy-start.2
  205.7 8.9 %convolution_convert_fusion = bf16[1024,384]{1,0:T(8,128)(2,1)S(1)} fusion(bf16[1024,4096]{0,1:T(8,128)(2,1)} %bitcast.2, bf16[4096,384]{0,1:T(8,128)(2,1)} %bitcast.140), kind=kOutput, calls=%fused_computation.21 | convolution fusion | flops 3221618688 | bytes 12320768 | tf_op jit(solution)/shard_map/dot_general | solution.py:93
  214.6 8.6 %collective-permute-start = (bf16[2,3,128]{2,1,0:T(4,128)(2,1)S(1)}, bf16[2,3,128]{2,1,0:T(4,128)(2,1)S(1)}, u32[]{:S(2)}, u32[]{:S(2)}) collective-permute-start(bf16[2,3,128]{2,1,0:T(4,128)(2,1)S(1)} %slice.51), channel_id=1, source_target_pairs={{0,32},{32,64},{64,96},{96,128},{128,160},{160,192},{192,224},{1,3... | collective-permute-start | bytes 4616 | tf_op jit(solution)/shard_map/ppermute | solution.py:14
  223.3 0.0 copy-done.3
  223.3 0.0 copy-done.2
  223.3 0.2 copy.34
  223.5 0.3 copy.32
  223.8 0.8 collective-permute-done
  224.6 0.2 copy.33
  224.7 0.4 maximum_convert_fusion
  225.1 1.2 fusion.14
  226.3 0.1 fusion.45
  226.4 0.1 pad_maximum_fusion
  226.4 1.8 copy.35
  228.2 6.6 %all-to-all-start.1 = ((f32[2,1024,128]{1,0,2:T(2,128)}), f32[2,1024,128]{1,0,2:T(2,128)}, u32[]{:S(2)}, u32[]{:S(2)}) async-start(f32[2,1024,128]{1,0,2:T(2,128)} %copy.35), calls=%async_computation.1 | async-start | bytes 2097152 | tf_op jit(solution)/shard_map/all_to_all | solution.py:60
  234.8 0.5 reduce-scatter.2.cloned.1.call-start
  235.3 0.3 fusion.62
  235.5 0.3 broadcast_multiply_fusion
  235.8 10.7 %all-to-all-done.1 = f32[2,1024,128]{1,0,2:T(2,128)} async-done(((f32[2,1024,128]{1,0,2:T(2,128)}), f32[2,1024,128]{1,0,2:T(2,128)}, u32[]{:S(2)}, u32[]{:S(2)}) %all-to-all-start.1) | async-done | bytes 1048608 | tf_op jit(solution)/shard_map/all_to_all | solution.py:60
  246.5 1.6 copy.36
  248.1 1.6 copy.37
  249.7 2.5 reshape.95
  252.2 0.0 copy-start.1
  252.2 3.2 fusion.70
  255.4 0.0 copy-done.1
  255.4 2.4 fusion
  257.8 3.9 fusion.4
  261.7 4.0 fusion.2
  265.7 3.9 subtract_bitcast_fusion
  269.7 3.9 add_bitcast_fusion
  273.5 0.5 multiply_subtract_fusion
  274.0 2.0 fusion.20
  276.0 2.2 fusion.24
  278.2 2.0 fusion.16
  280.2 2.1 add_bitcast_fusion.1
  282.4 1.3 fusion.27
  283.7 2.1 fusion.19
  285.8 0.0 copy-start.4
  285.8 1.2 all_to_all.32
  287.0 0.3 copy.44
  287.3 12.6 %all_to_all.39 = f32[8,1024,16]{1,2,0:T(8,128)S(1)} all-to-all(f32[8,1024,16]{1,2,0:T(8,128)S(1)} %copy.44), channel_id=1, replica_groups=mesh['seq'=8,'chan'=32] {'seq'}, dimensions={0} | all-to-all | bytes 1048576 | tf_op jit(solution)/shard_map/all_to_all | solution.py:86
  299.9 0.0 copy-done.4
  299.9 0.1 fusion.30
  300.1 0.0 copy-done
  300.1 8.1 %fusion.142 = f32[1024,4096]{1,0:T(8,128)} fusion(bf16[1024,128]{0,1:T(8,128)(2,1)S(1)} %fusion.30, bf16[128,4096]{1,0:T(8,128)(2,1)S(1)} %copy-done), kind=kOutput, calls=%fused_computation.161 | convolution fusion | flops 1073741824 | bytes 18087936 | tf_op jit(solution)/shard_map/dot_general | solution.py:112
  308.2 0.0 reduce-scatter.2.cloned.1.call-update
  308.2 162.5 %reduce-scatter.2.cloned.1.call-done = f32[1024,128]{1,0:T(8,128)} async-done(((f32[1024,4096]{1,0:T(8,128)}), f32[1024,128]{1,0:T(8,128)}) %reduce-scatter.2.cloned.1.call-update) | async-done | bytes 524304 | tf_op jit(solution)/shard_map/reduce_scatter | solution.py:113
  470.7 1.8 convert_element_type.67
  (3 shorter events, 0.0 us)
Async XLA Ops:
  6.5 293.5 %copy-start = (bf16[128,4096]{1,0:T(8,128)(2,1)S(1)}, bf16[128,4096]{1,0:T(8,128)(2,1)}, u32[]{:S(2)}) copy-start(bf16[128,4096]{1,0:T(8,128)(2,1)} %param.11) | copy-start | bytes 3145732
  12.0 193.7 %all-to-all-start = ((bf16[32,1024,128]{1,2,0:T(8,128)(2,1)}), bf16[32,1024,128]{1,2,0:T(8,128)(2,1)}, u32[]{:S(2)}, u32[]{:S(2)}) async-start(bf16[32,1024,128]{1,2,0:T(8,128)(2,1)} %stack.6), calls=%async_computation | async-start | bytes 16777216 | tf_op jit(solution)/shard_map/all_to_all | solution.py:95
  205.7 17.5 %copy-start.3 = (f32[3,3,128]{2,1,0:T(4,128)S(1)}, f32[3,3,128]{2,1,0:T(4,128)}, u32[]{:S(2)}) copy-start(f32[3,3,128]{2,1,0:T(4,128)} %param.8) | copy-start | bytes 13828
  205.7 17.6 %copy-start.2 = (f32[1024,128]{1,0:T(8,128)S(1)}, f32[1024,128]{1,0:T(8,128)}, u32[]{:S(2)}) copy-start(f32[1024,128]{1,0:T(8,128)} %param.9) | copy-start | bytes 1572868
  214.6 9.9 %collective-permute-start = (bf16[2,3,128]{2,1,0:T(4,128)(2,1)S(1)}, bf16[2,3,128]{2,1,0:T(4,128)(2,1)S(1)}, u32[]{:S(2)}, u32[]{:S(2)}) collective-permute-start(bf16[2,3,128]{2,1,0:T(4,128)(2,1)S(1)} %slice.51), channel_id=1, source_target_pairs={{0,32},{32,64},{64,96},{96,128},{128,160},{160,192},{192,224},{1,3... | collective-permute-start | bytes 4616 | tf_op jit(solution)/shard_map/ppermute | solution.py:14
  228.2 18.3 %all-to-all-start.1 = ((f32[2,1024,128]{1,0,2:T(2,128)}), f32[2,1024,128]{1,0,2:T(2,128)}, u32[]{:S(2)}, u32[]{:S(2)}) async-start(f32[2,1024,128]{1,0,2:T(2,128)} %copy.35), calls=%async_computation.1 | async-start | bytes 2097152 | tf_op jit(solution)/shard_map/all_to_all | solution.py:60
  234.8 235.9 %reduce-scatter.2.cloned.1.call-start = ((), (), s32[]{:S(2)}) async-start(), calls=%async_computation.4 | async-start | bytes 17301504 | tf_op jit(solution)/shard_map/reduce_scatter | solution.py:113
  252.2 3.2 copy-start.1
  285.8 14.1 %copy-start.4 = (f32[128]{0:T(128)S(1)}, f32[128]{0:T(128)}, u32[]{:S(2)}) copy-start(f32[128]{0:T(128)} %param.10) | copy-start | bytes 1540
Sparse Core Ops, SparseCore 0:
  308.3 162.3 reduce-scatter.1
